TPU v7x, 256 devices: a whole 4x4x8 slice. The times are simulated.
256 devices in a mesh: dp: 32 (over z, x), seq: 8 (over y, core).
Axes of the slice: x: 4, y: 4, z: 8, core: 2. Of those that a mesh axis runs over, the one named last changes fastest.
Arguments:
- hidden: bfloat16 [32, 6144, 2560], P('dp', 'seq'), may hold values from -6 to 6
- log_decay: float32 [32, 40, 6144], P('dp', None, 'seq'), may hold values from -2 to 0, as said below
- input_weight: bfloat16 [2816, 2560], P(('dp', 'seq')), may hold values from -0.125 to 0.125
- conv_weight: bfloat16 [4, 2816], replicated, may hold values from -3 to 3
- conv_bias: float32 [2816], replicated, may hold values from -0.5 to 0.5
- skip_gain: float32 [40], replicated, may hold values from 0.5 to 1.5
Outputs:
- mixer_out: bfloat16 [32, 6144, 2560], P('dp', 'seq')
Inputs may be any that keep to these rules, and one draw needn't show every extreme that they name: `log_decay`: every value is negative.
All inputs are finite; a program needn't handle non-finite values.
Results may differ from a plain program's by a relative error of at most 0.0064.
Values may be sent and summed in bfloat16 or wider, within the bound.
No kernel may reach another device: no remote copies, remote signals or barrier semaphores. Data moves between devices by JAX's collectives and lax.ppermute only.
A program may use at most 128 MiB of HBM per device.

v0:
```python
import jax
import jax.numpy as jnp
from jax import lax
from jax.sharding import Mesh, PartitionSpec as P

HALF_HEADS = 40
HEAD_DIM = 64
STATE = 128
SPAN = 256
CONV = 4
INNER = 2560
COLS = 2816


def mixing_output(x_heads, b_span, c_span, cumulative, step_size):
    scores = jnp.dot(c_span, b_span.T, preferred_element_type=jnp.float32)
    span_len = cumulative.shape[1]
    causal = jnp.arange(span_len)[:, None] >= jnp.arange(span_len)[None, :]
    spread = jnp.where(causal[None], cumulative[:, :, None] - cumulative[:, None, :], -jnp.inf)
    mixing = (scores[None] * jnp.exp(spread) * step_size[:, None, :]).astype(jnp.bfloat16)
    return jnp.einsum("hqk,khp->qhp", mixing, x_heads, preferred_element_type=jnp.float32)


def span_state(x_heads, b_span, cumulative, step_size):
    weight = jnp.exp(cumulative[:, -1:] - cumulative) * step_size
    decayed = (x_heads * weight.T[:, :, None]).astype(jnp.bfloat16)
    return jnp.einsum("khp,kn->hpn", decayed, b_span, preferred_element_type=jnp.float32)


def state_output(c_span, entering, cumulative):
    readout = jnp.einsum(
        "qn,hpn->qhp", c_span.astype(jnp.float32), entering, precision=lax.Precision.HIGHEST
    )
    return jnp.exp(cumulative).T[:, :, None] * readout


SEQ = ("y", "core")


def shifted(array, by):
    peers = lax.axis_size(SEQ)
    pairs = [(i, i + by) for i in range(peers) if i + by < peers]
    return lax.ppermute(array, SEQ, pairs)


def scan_entering(total, state):
    acc_total, acc_state = (shifted(total, 1), shifted(state, 1))
    by = 1
    while by < lax.axis_size(SEQ):
        got_total, got_state = (shifted(acc_total, by), shifted(acc_state, by))
        acc_state = jnp.exp(acc_total)[:, None, None] * got_state + acc_state
        acc_total = acc_total + got_total
        by *= 2
    return acc_state


def project(token_rows, input_weight):
    rows = input_weight.shape[0]
    mine = lax.all_gather(input_weight, ("dp", "y"), axis=0, tiled=True)
    other = lax.ppermute(mine, "core", [(0, 1), (1, 0)])
    dims = (((1,), (1,)), ((), ()))
    p_mine = lax.dot_general(token_rows, mine, dims, preferred_element_type=jnp.float32).astype(
        jnp.bfloat16
    )
    p_other = lax.dot_general(token_rows, other, dims, preferred_element_type=jnp.float32).astype(
        jnp.bfloat16
    )
    first = lax.axis_index("core") == 0
    p0 = jnp.where(first, p_mine, p_other)
    p1 = jnp.where(first, p_other, p_mine)
    length = token_rows.shape[0]
    groups = mine.shape[0] // rows
    return jnp.stack(
        [p0.reshape(length, groups, rows), p1.reshape(length, groups, rows)], axis=2
    ).reshape(length, COLS)


def body(hidden, log_decay, input_weight, conv_weight, conv_bias, skip_gain):
    token_rows = hidden[0]
    length = token_rows.shape[0]
    projected = project(token_rows, input_weight)
    last_rows = projected[length - (CONV - 1) :]
    before_rows = shifted(last_rows, 1)
    extended = jnp.concatenate([before_rows, projected], axis=0)
    filtered = jnp.broadcast_to(conv_bias[None, :], (length, COLS))
    for kernel_tap in range(CONV):
        filtered = (
            filtered
            + extended[kernel_tap : kernel_tap + length].astype(jnp.float32)
            * conv_weight[kernel_tap].astype(jnp.float32)[None, :]
        )
    active = jax.nn.silu(filtered).astype(jnp.bfloat16)
    span_count = length // SPAN
    x_all = active[:, :INNER].reshape(span_count, SPAN, HALF_HEADS, HEAD_DIM)
    b_all = active[:, INNER : INNER + STATE].reshape(span_count, SPAN, STATE)
    c_all = active[:, INNER + STATE :].reshape(span_count, SPAN, STATE)
    decay_spans = log_decay[0].reshape(HALF_HEADS, span_count, SPAN).transpose(1, 0, 2)
    cumulative = jnp.cumsum(decay_spans, axis=2)
    steps_all = -decay_spans
    totals = cumulative[:, :, -1]
    device_total = jnp.sum(totals, axis=0)
    zero_state = jnp.zeros((HALF_HEADS, HEAD_DIM, STATE), jnp.float32)

    def state_of(inputs):
        x_heads, b_span, cum_span, step_span = inputs
        return span_state(x_heads, b_span, cum_span, step_span)

    states = lax.map(state_of, (x_all, b_all, cumulative, steps_all))

    def gather_local(held_state, inputs):
        span_total, state_piece = inputs
        return (jnp.exp(span_total)[:, None, None] * held_state + state_piece, None)

    local_end, _ = lax.scan(gather_local, zero_state, (totals, states))
    entering_dev = scan_entering(device_total, local_end)

    def emit(held_state, inputs):
        x_heads, b_span, c_span, cum_span, step_span, span_total, state_piece = inputs
        outputs = mixing_output(x_heads, b_span, c_span, cum_span, step_span) + state_output(
            c_span, held_state, cum_span
        )
        return (jnp.exp(span_total)[:, None, None] * held_state + state_piece, outputs)

    _, outputs = lax.scan(
        emit, entering_dev, (x_all, b_all, c_all, cumulative, steps_all, totals, states)
    )
    outputs = outputs.reshape(length, HALF_HEADS, HEAD_DIM)
    final = outputs + skip_gain[None, :, None] * x_all.reshape(length, HALF_HEADS, HEAD_DIM).astype(
        jnp.float32
    )
    return final.reshape(1, length, INNER).astype(jnp.bfloat16)


def solution(mesh):
    split = Mesh(
        mesh.devices.reshape(mesh.shape["dp"], mesh.shape["seq"] // 2, 2), ("dp", "y", "core")
    )
    placed = (P("dp", SEQ, None), P("dp", None, SEQ), P(("dp",) + SEQ, None), P(), P(), P())
    return jax.shard_map(
        body, mesh=split, in_specs=placed, out_specs=P("dp", SEQ, None), check_vma=False
    )
```

profile of v0, /device:TPU:8, one launch (start us, length us, event | category | flops | bytes accessed | tf_op | source)
XLA Modules:
  0.0 609.2 jit_solution(4100899505798613028)
XLA Ops:
  6.5 0.7 all-gather.3.cloned.1.call-update
  7.3 136.0 %all-gather.3.cloned.1.call-done = bf16[128,11,2560]{2,1,0:T(8,128)(2,1)} async-done(((bf16[1,11,2560]{2,1,0:T(8,128)(2,1)}), bf16[128,11,2560]{2,1,0:T(8,128)(2,1)}) %all-gather.3.cloned.1.call-update) | async-done | bytes 7208976 | tf_op jit(solution)/shard_map/all_gather | solution.py:59
  143.3 13.2 %reshape.82 = bf16[1408,2560]{1,0:T(8,128)(2,1)} reshape(bf16[128,11,2560]{2,1,0:T(8,128)(2,1)} %all-gather.3.cloned.1.call-done) | data formatting | bytes 14417920
  156.6 1.8 reduce-window.6
  158.9 10.3 %fusion.40 = bf16[768,1408]{1,0:T(8,128)(2,1)S(1)} fusion(bf16[1408,2560]{1,0:T(8,128)(2,1)} %reshape.82, bf16[1,768,2560]{2,1,0:T(8,128)(2,1)} %param.12), kind=kOutput, calls=%fused_computation.64 | convolution fusion | flops 5537562624 | bytes 13303808 | tf_op jit(solution)/shard_map/dot_general | solution.py:62
  169.3 10.6 %broadcast_select_fusion = (bf16[768,1408]{1,0:T(8,128)(2,1)}, bf16[768,1408]{1,0:T(8,128)(2,1)S(1)}) fusion(bf16[768,1408]{1,0:T(8,128)(2,1)S(1)} %fusion.40, pred[]{:T(512)S(6)} %eq.3, bf16[1408,2560]{1,0:T(8,128)(2,1)} %collective-permute-done.3, bf16[1,768,2560]{2,1,0:T(8,128)(2,1)S(1)} %copy-done.5), kind=kOutput, calls=%fused_computation.66 | convolution fusion | flops 5539725312 | bytes 17629184 | tf_op jit(solution)/shard_map/dot_general | solution.py:65
  179.8 2.5 copy.56
  182.3 2.8 stack_reshape.6
  185.1 1.9 constant_dynamic-update-slice_fusion.1
  186.9 4.2 copy.57
  191.2 2.8 stack_reshape.7
  193.9 1.9 constant_dynamic-update-slice_fusion
  195.8 1.6 slice.67
  197.4 2.0 copy.58
  199.7 2.6 collective-permute-start.4
  202.5 6.4 %copy.59 = bf16[768,128,2,11]{0,3,2,1:T(8,128)(2,1)} copy(bf16[768,128,2,11]{0,3,1,2:T(8,128)(2,1)} %constant_dynamic-update-slice_fusion) | data formatting | bytes 8650752 | tf_op jit(solution)/shard_map/stack | solution.py:73
  208.9 7.7 %reshape.72 = bf16[768,2816]{0,1:T(8,128)(2,1)} reshape(bf16[768,128,2,11]{0,3,2,1:T(8,128)(2,1)} %copy.59) | data formatting | bytes 8650752 | tf_op jit(solution)/shard_map/reshape | solution.py:75
  216.6 0.4 copy.60
  217.0 15.4 %multiply_convert_fusion.5 = bf16[768,2816]{0,1:T(8,128)(2,1)S(1)} fusion(bf16[768,2816]{0,1:T(8,128)(2,1)} %reshape.72, bf16[3,2816]{0,1:T(8,128)(2,1)S(1)} %copy.60, f32[2816]{0:T(1024)S(1)} %get-tuple-element.197, f32[2816]{0:T(1024)S(1)} %get-tuple-element.198, f32[2816]{0:T(1024)S(1)} %get-tuple-element.196, f32[2816]{0:T(1024)S(1)} %get-tuple-element.195, ...), kind=kLoop, calls=%fused_computation.50 | loop fusion | flops 56229888 | bytes 8723968 | tf_op jit(solution)/shard_map/convert_element_type | solution.py:92
  232.5 0.8 fusion.47
  233.2 2.5 slice.72
  235.9 11.3 %reshape.73 = bf16[3,256,40,64]{1,0,3,2:T(4,128)(2,1)} reshape(bf16[768,2560]{0,1:T(8,128)(2,1)} %slice.72) | data formatting | bytes 7864320 | tf_op jit(solution)/shard_map/reshape | solution.py:94
  247.2 5.2 copy.62
  252.4 9.8 %while.33 = (s32[]{:T(128)}, f32[3,40,64,128]{3,2,1,0:T(8,128)}, bf16[3,256,40,64]{1,3,2,0:T(8,128)(2,1)}, f32[3,40,256]{2,1,0:T(8,128)S(1)}, f32[3,40,256]{2,0,...) while((s32[]{:T(128)}, f32[3,40,64,128]{3,2,1,0:T(8,128)}, bf16[3,256,40,64]{1,3,2,0:T(8,128)(2,1)}, ...), condition=%wide.region_4.5_spmd, body=%wide.region_3.4_spmd.sunk | while | flops 169758720 | bytes 3262517 | solution.py:108
  252.7 2.9 fusion.67
  256.0 2.9 fusion.67
  259.3 2.9 fusion.67
  262.2 4.7 while.35
  262.2 1.5 bitcast_add_fusion.6
  263.7 1.5 bitcast_add_fusion.6
  265.3 1.5 bitcast_add_fusion.6
  266.9 3.0 collective-permute-start.5
  269.9 15.9 %collective-permute-done.5 = f32[40,64,128]{2,1,0:T(8,128)S(1)} collective-permute-done((f32[40,64,128]{2,1,0:T(8,128)S(1)}, f32[40,64,128]{2,1,0:T(8,128)S(1)}, u32[]{:S(2)}, u32[]{:S(2)}) %collective-permute-start.5) | collective-permute-done | bytes 1310752 | tf_op jit(solution)/shard_map/ppermute | solution.py:43
  285.8 1.9 collective-permute-start.6
  287.7 3.5 collective-permute-start
  291.2 13.5 %collective-permute-done = f32[40]{0:T(128)S(1)} collective-permute-done((f32[40]{0:T(128)S(1)}, f32[40]{0:T(128)S(1)}, u32[]{:S(2)}, u32[]{:S(2)}) %collective-permute-start) | collective-permute-done | bytes 192 | tf_op jit(solution)/shard_map/ppermute | solution.py:43
  304.8 1.9 collective-permute-start.1
  306.7 2.9 collective-permute-done.1
  309.9 3.4 collective-permute-start.7
  313.3 28.5 %collective-permute-done.7 = f32[40,64,128]{2,1,0:T(8,128)S(1)} collective-permute-done((f32[40,64,128]{2,1,0:T(8,128)S(1)}, f32[40,64,128]{2,1,0:T(8,128)S(1)}, u32[]{:S(2)}, u32[]{:S(2)}) %collective-permute-start.7) | collective-permute-done | bytes 1310752 | tf_op jit(solution)/shard_map/ppermute | solution.py:43
  342.0 2.9 collective-permute-start.8
  345.0 2.1 collective-permute-start.2
  347.3 26.7 %collective-permute-done.2 = f32[40]{0:T(128)S(1)} collective-permute-done((f32[40]{0:T(128)S(1)}, f32[40]{0:T(128)S(1)}, u32[]{:S(2)}, u32[]{:S(2)}) %collective-permute-start.2) | collective-permute-done | bytes 192 | tf_op jit(solution)/shard_map/ppermute | solution.py:43
  374.0 1.1 copy.65
  375.1 1.3 multiply_add_fusion
  376.3 209.5 %while.34 = (s32[]{:T(128)}, f32[40,64,128]{2,1,0:T(8,128)}, f32[3,256,40,64]{1,0,3,2:T(4,128)}, f32[3,40]{1,0:T(4,128)S(1)}, f32[3,40,64,128]{3,2,1,0:T(8,128)}...) while((s32[]{:T(128)}, f32[40,64,128]{2,1,0:T(8,128)}, ...), condition=%wide.region_8.9_spmd, body=%wide.region_7.8_spmd.sunk | while | flops 1374093312 | bytes 26208364 | solution.py:124
  376.3 2.5 fusion.74
  379.2 4.3 fusion.76
  383.5 2.9 copy.94
  386.4 56.8 %dynamic_update_slice.12 = f32[3,256,40,64]{1,0,3,2:T(4,128)} dynamic-update-slice(f32[3,256,40,64]{1,0,3,2:T(4,128)} %get-tuple-element.428, f32[1,256,40,64]{1,0,3,2:T(1,128)S(1)} %copy.94, s32[]{:T(128)} %get-tuple-element.426, s32[]{:T(128)} %constant.52.clone.1..sunk, s32[]{:T(128)} %constant.52.clone.1..sunk, s32[]{:T(128)} %constant.52.clone.1..sunk) | dynamic-update-slice | bytes 5242884 | tf_op jit(solution)/shard_map/while/body/jit(dynamic_update_index_in_dim)/dynamic_update_slice | solution.py:124
  443.2 3.0 bitcast_add_fusion.5
  446.2 2.5 fusion.74
  449.0 4.3 fusion.76
  453.3 2.9 copy.94
  456.2 56.8 %dynamic_update_slice.12 = f32[3,256,40,64]{1,0,3,2:T(4,128)} dynamic-update-slice(f32[3,256,40,64]{1,0,3,2:T(4,128)} %get-tuple-element.428, f32[1,256,40,64]{1,0,3,2:T(1,128)S(1)} %copy.94, s32[]{:T(128)} %get-tuple-element.426, s32[]{:T(128)} %constant.52.clone.1..sunk, s32[]{:T(128)} %constant.52.clone.1..sunk, s32[]{:T(128)} %constant.52.clone.1..sunk) | dynamic-update-slice | bytes 5242884 | tf_op jit(solution)/shard_map/while/body/jit(dynamic_update_index_in_dim)/dynamic_update_slice | solution.py:124
  513.0 3.0 bitcast_add_fusion.5
  516.0 2.5 fusion.74
  518.8 4.3 fusion.76
  523.1 2.9 copy.94
  526.1 56.8 %dynamic_update_slice.12 = f32[3,256,40,64]{1,0,3,2:T(4,128)} dynamic-update-slice(f32[3,256,40,64]{1,0,3,2:T(4,128)} %get-tuple-element.428, f32[1,256,40,64]{1,0,3,2:T(1,128)S(1)} %copy.94, s32[]{:T(128)} %get-tuple-element.426, s32[]{:T(128)} %constant.52.clone.1..sunk, s32[]{:T(128)} %constant.52.clone.1..sunk, s32[]{:T(128)} %constant.52.clone.1..sunk) | dynamic-update-slice | bytes 5242884 | tf_op jit(solution)/shard_map/while/body/jit(dynamic_update_index_in_dim)/dynamic_update_slice | solution.py:124
  582.8 3.0 bitcast_add_fusion.5
  585.8 5.9 copy.81
  591.8 4.3 fusion.35
  596.0 6.3 %copy.69 = bf16[1,768,2560]{2,1,0:T(8,128)(2,1)} copy(bf16[1,768,2560]{1,2,0:T(8,128)(2,1)} %fusion.35) | data formatting | bytes 7864320 | tf_op jit(solution)/shard_map/convert_element_type | solution.py:131
  (81 shorter events, 3.9 us)
Async XLA Ops:
  6.5 136.7 %all-gather.3.cloned.1.call-start = ((), (), s32[]{:S(2)}) async-start(), calls=%async_computation | async-start | bytes 10567680 | tf_op jit(solution)/shard_map/all_gather | solution.py:59
  7.3 149.2 %copy-start.1 = (f32[1,40,768]{2,1,0:T(8,128)S(1)}, f32[1,40,768]{2,1,0:T(8,128)}, u32[]{:S(2)}) copy-start(f32[1,40,768]{2,1,0:T(8,128)} %param.13) | copy-start | bytes 368644
  7.3 151.4 %copy-start.2 = (bf16[4,2816]{1,0:T(4,128)(2,1)S(1)}, bf16[4,2816]{1,0:T(4,128)(2,1)}, u32[]{:S(2)}) copy-start(bf16[4,2816]{1,0:T(4,128)(2,1)} %param.15) | copy-start | bytes 67588
  156.4 12.8 %collective-permute-start.3 = (bf16[1408,2560]{1,0:T(8,128)(2,1)}, bf16[1408,2560]{1,0:T(8,128)(2,1)}, u32[]{:S(2)}, u32[]{:S(2)}) collective-permute-start(bf16[1408,2560]{1,0:T(8,128)(2,1)} %reshape.82), channel_id=1, source_target_pairs={{0,1},{1,0},{2,3},{3,2},{4,5},{5,4},{6,7},{7,6},{8,9},{9,8},{10,11... | collective-permute-start | bytes 21626888 | tf_op jit(solution)/shard_map/ppermute | solution.py:60
  158.9 10.3 %copy-start.5 = (bf16[1,768,2560]{2,1,0:T(8,128)(2,1)S(1)}, bf16[1,768,2560]{2,1,0:T(8,128)(2,1)}, u32[]{:S(2)}) copy-start(bf16[1,768,2560]{2,1,0:T(8,128)(2,1)} %param.12) | copy-start | bytes 11796484
  199.7 17.0 %collective-permute-start.4 = (bf16[3,2816]{1,0:T(4,128)(2,1)S(1)}, bf16[3,2816]{1,0:T(4,128)(2,1)S(1)}, u32[]{:S(2)}, u32[]{:S(2)}) collective-permute-start(bf16[3,2816]{1,0:T(4,128)(2,1)S(1)} %slice.52), channel_id=1, source_target_pairs={{0,1},{1,2},{2,3},{3,4},{4,5},{5,6},{6,7},{8,9},{9,10},{10,11},{11... | collective-permute-start | bytes 50696 | tf_op jit(solution)/shard_map/ppermute | solution.py:43
  208.9 8.1 %copy-start.3 = (f32[2816]{0:T(1024)S(1)}, f32[2816]{0:T(1024)}, u32[]{:S(2)}) copy-start(f32[2816]{0:T(1024)} %param.16) | copy-start | bytes 33796
  232.4 3.3 copy-start
  266.9 18.9 %collective-permute-start.5 = (f32[40,64,128]{2,1,0:T(8,128)S(1)}, f32[40,64,128]{2,1,0:T(8,128)S(1)}, u32[]{:S(2)}, u32[]{:S(2)}) collective-permute-start(f32[40,64,128]{2,1,0:T(8,128)S(1)} %get-tuple-element.112), channel_id=1, source_target_pairs={{0,1},{1,2},{2,3},{3,4},{4,5},{5,6},{6,7},{8,9},{9,10},{10,11},{11... | collective-permute-start | bytes 3932168 | tf_op jit(solution)/shard_map/ppermute | solution.py:43
  285.8 23.8 %collective-permute-start.6 = (f32[40,64,128]{2,1,0:T(8,128)S(1)}, f32[40,64,128]{2,1,0:T(8,128)S(1)}, u32[]{:S(2)}, u32[]{:S(2)}) collective-permute-start(f32[40,64,128]{2,1,0:T(8,128)S(1)} %collective-permute-done.5), channel_id=1, source_target_pairs={{0,1},{1,2},{2,3},{3,4},{4,5},{5,6},{6,7},{8,9},{9,10},{10,11},{11... | collective-permute-start | bytes 3932168 | tf_op jit(solution)/shard_map/ppermute | solution.py:43
  287.7 17.1 %collective-permute-start = (f32[40]{0:T(128)S(1)}, f32[40]{0:T(128)S(1)}, u32[]{:S(2)}, u32[]{:S(2)}) collective-permute-start(f32[40]{0:T(128)S(1)} %get-tuple-element.193), channel_id=1, source_target_pairs={{0,1},{1,2},{2,3},{3,4},{4,5},{5,6},{6,7},{8,9},{9,10},{10,11},{11... | collective-permute-start | bytes 488 | tf_op jit(solution)/shard_map/ppermute | solution.py:43
  304.8 4.8 collective-permute-start.1
  309.6 37.5 %copy-start.4 = (f32[40]{0:T(128)S(1)}, f32[40]{0:T(128)}, u32[]{:S(2)}) copy-start(f32[40]{0:T(128)} %param.17) | copy-start | bytes 484
  309.9 31.9 %collective-permute-start.7 = (f32[40,64,128]{2,1,0:T(8,128)S(1)}, f32[40,64,128]{2,1,0:T(8,128)S(1)}, u32[]{:S(2)}, u32[]{:S(2)}) collective-permute-start(f32[40,64,128]{2,1,0:T(8,128)S(1)} %multiply_add_fusion.2), channel_id=1, source_target_pairs={{0,2},{1,3},{2,4},{3,5},{4,6},{5,7},{8,10},{9,11},{10,12},{11,13},... | collective-permute-start | bytes 3932168 | tf_op jit(solution)/shard_map/ppermute | solution.py:43
  342.0 33.0 %collective-permute-start.8 = (f32[40,64,128]{2,1,0:T(8,128)S(1)}, f32[40,64,128]{2,1,0:T(8,128)S(1)}, u32[]{:S(2)}, u32[]{:S(2)}) collective-permute-start(f32[40,64,128]{2,1,0:T(8,128)S(1)} %multiply_add_fusion.1), channel_id=1, source_target_pairs={{0,4},{1,5},{2,6},{3,7},{8,12},{9,13},{10,14},{11,15},{16,20},{17,... | collective-permute-start | bytes 3932168 | tf_op jit(solution)/shard_map/ppermute | solution.py:43
  345.0 29.0 %collective-permute-start.2 = (f32[40]{0:T(128)S(1)}, f32[40]{0:T(128)S(1)}, u32[]{:S(2)}, u32[]{:S(2)}) collective-permute-start(f32[40]{0:T(128)S(1)} %get-tuple-element.242), channel_id=1, source_target_pairs={{0,2},{1,3},{2,4},{3,5},{4,6},{5,7},{8,10},{9,11},{10,12},{11,13},... | collective-permute-start | bytes 488 | tf_op jit(solution)/shard_map/ppermute | solution.py:43
Sparse Core Ops, SparseCore 0:
  10.8 132.3 all-gather.2
where the time goes:
time: 615 us; the launch traced here: 609 us
  local copies, waits for them, and re-layouts  262 us (43%)
  waiting for transfers between devices  224 us (36%)
  matrix products  50.5 us (8%)
  other arithmetic  37.4 us (6%)
  starting transfers between devices  21.4 us (3%)
  between operations  13.7 us (2%)
    dynamic_update_slice x6, local copies, waits for them, and re-layouts, body(): lax.scan(emit, entering_dev, (x_all, b_all, c_all, cumulative, steps_all,...  179 us
    all_gather x1, waiting for transfers between devices, project(): mine = lax.all_gather(input_weight, ('dp', 'y'), axis=0, tiled=True)  136 us
    ppermute x8, waiting for transfers between devices, shifted(): return lax.ppermute(array, SEQ, pairs)  87.6 us
    ppermute x8, starting transfers between devices, shifted(): return lax.ppermute(array, SEQ, pairs)  21.4 us
    unnamed x15, local copies, waits for them, and re-layouts  21 us
    convert_element_type x1, other arithmetic, body(): active = jax.nn.silu(filtered).astype(jnp.bfloat16)  15.4 us
    another operation x4, local copies, waits for them, and re-layouts, project(): jnp.stack([p0.reshape(length, groups, rows), p1.reshape(length, groups, r...  13.8 us
    dot_general x3, matrix products, mixing_output(): jnp.einsum('hqk,khp->qhp', mixing, x_heads, preferred_element_type=jnp.fl...  12.8 us
  transfers between devices with their start and end apart: 10, of which 6 were waited for; matrix products, arithmetic and copies ran while one was open for 5% of the time, Pallas kernels for 0%

commit v1 on v0

--- a/solution.py
+++ b/solution.py
@@ -56,7 +56,10 @@
 
 def project(token_rows, input_weight):
     rows = input_weight.shape[0]
-    mine = lax.all_gather(input_weight, ("dp", "y"), axis=0, tiled=True)
+    mine = jnp.concatenate(
+        lax.all_to_all(jnp.stack([input_weight] * lax.axis_size(("dp", "y"))), ("dp", "y"), 0, 0),
+        axis=0,
+    )
     other = lax.ppermute(mine, "core", [(0, 1), (1, 0)])
     dims = (((1,), (1,)), ((), ()))
     p_mine = lax.dot_general(token_rows, mine, dims, preferred_element_type=jnp.float32).astype(

time: 615 us -> 716 us (1.16)
  blocking collectives: 0 us -> 247 us
  waiting for transfers between devices: 224 us -> 91.2 us
  between operations: 13.7 us -> 0.3 us
    all_to_all x0 -> x1, blocking collectives: none -> 247 us  [project(): lax.all_to_all(jnp.stack([input_weight] * lax.axis_size(('dp', 'y'))), ('...]
    all_gather x1 -> x0, waiting for transfers between devices: 136 us -> none  [project(): mine = lax.all_gather(input_weight, ('dp', 'y'), axis=0, tiled=True)]
    reshape x2 -> x3, local copies, waits for them, and re-layouts: 0.12 us -> 13.3 us  [the longest x1 13.2 us: project(): jnp.concatenate(lax.all_to_all(jnp.stack([input_weight] * lax.axis_size((...]
    unnamed x15 -> x14, local copies, waits for them, and re-layouts: 21 us -> 7.85 us
  transfers between devices with their start and end apart: 10 -> 9, of which waited for: 6 -> 5; matrix products, arithmetic and copies ran while one was open for 5% -> 4% of each run, Pallas kernels for 0% -> 0%
where the time goes in v1:
time: 716 us; the launch traced here: 709 us
  local copies, waits for them, and re-layouts  264 us (37%)
  blocking collectives  247 us (34%)
  waiting for transfers between devices  91.2 us (13%)
  matrix products  50.5 us (7%)
  other arithmetic  37.4 us (5%)
  starting transfers between devices  18.8 us (3%)
    all_to_all x1, blocking collectives, project(): lax.all_to_all(jnp.stack([input_weight] * lax.axis_size(('dp', 'y'))), ('...  247 us
    dynamic_update_slice x6, local copies, waits for them, and re-layouts, body(): lax.scan(emit, entering_dev, (x_all, b_all, c_all, cumulative, steps_all,...  179 us
    ppermute x8, waiting for transfers between devices, shifted(): return lax.ppermute(array, SEQ, pairs)  91.2 us
    ppermute x8, starting transfers between devices, shifted(): return lax.ppermute(array, SEQ, pairs)  18.8 us
    convert_element_type x1, other arithmetic, body(): active = jax.nn.silu(filtered).astype(jnp.bfloat16)  15.4 us
  transfers between devices with their start and end apart: 9, of which 5 were waited for; matrix products, arithmetic and copies ran while one was open for 4% of the time, Pallas kernels for 0%

profile of v1, /device:TPU:8, one launch (start us, length us, event | category | flops | bytes accessed | tf_op | source)
XLA Modules:
  0.0 709.3 jit_solution(8490689134180259980)
XLA Ops:
  0.0 2.2 stack.4
  2.2 247.1 %all_to_all.5 = bf16[128,11,2560]{2,1,0:T(8,128)(2,1)} all-to-all(bf16[128,11,2560]{2,1,0:T(8,128)(2,1)S(1)} %stack.4), channel_id=1, replica_groups=mesh['dp'=32,'y'=4,'core'=2] {'dp','y'}, dimensions={0} | all-to-all | bytes 14417920 | tf_op jit(solution)/shard_map/all_to_all | solution.py:60
  249.3 13.2 %reshape.77 = bf16[1408,2560]{1,0:T(8,128)(2,1)} reshape(bf16[128,11,2560]{2,1,0:T(8,128)(2,1)} %all_to_all.5) | data formatting | bytes 14417920 | tf_op jit(solution)/shard_map/reshape | solution.py:59
  262.7 1.8 reduce-window.6
  265.0 10.3 %fusion.40 = bf16[768,1408]{1,0:T(8,128)(2,1)S(1)} fusion(bf16[1408,2560]{1,0:T(8,128)(2,1)} %reshape.77, bf16[1,768,2560]{2,1,0:T(8,128)(2,1)} %param.12), kind=kOutput, calls=%fused_computation.64 | convolution fusion | flops 5537562624 | bytes 13303808 | tf_op jit(solution)/shard_map/dot_general | solution.py:65
  275.4 10.6 %broadcast_select_fusion = (bf16[768,1408]{1,0:T(8,128)(2,1)}, bf16[768,1408]{1,0:T(8,128)(2,1)S(1)}) fusion(bf16[768,1408]{1,0:T(8,128)(2,1)S(1)} %fusion.40, pred[]{:T(512)S(6)} %eq.3, bf16[1408,2560]{1,0:T(8,128)(2,1)} %collective-permute-done.3, bf16[1,768,2560]{2,1,0:T(8,128)(2,1)S(1)} %copy-done.5), kind=kOutput, calls=%fused_computation.66 | convolution fusion | flops 5539725312 | bytes 17629184 | tf_op jit(solution)/shard_map/dot_general | solution.py:68
  285.9 2.6 copy.38
  288.5 2.8 stack_reshape.6
  291.3 1.9 constant_dynamic-update-slice_fusion.1
  293.1 4.1 copy.39
  297.3 2.8 stack_reshape.7
  300.0 1.9 constant_dynamic-update-slice_fusion
  301.9 1.6 slice.67
  303.5 2.0 copy.40
  305.8 2.6 collective-permute-start.4
  308.6 6.4 copy.41
  315.0 7.7 %reshape.78 = bf16[768,2816]{0,1:T(8,128)(2,1)} reshape(bf16[768,128,2,11]{0,3,2,1:T(8,128)(2,1)} %copy.41) | data formatting | bytes 8650752 | tf_op jit(solution)/shard_map/reshape | solution.py:78
  322.7 0.4 copy.42
  323.1 15.4 %multiply_convert_fusion.5 = bf16[768,2816]{0,1:T(8,128)(2,1)S(1)} fusion(bf16[768,2816]{0,1:T(8,128)(2,1)} %reshape.78, bf16[3,2816]{0,1:T(8,128)(2,1)S(1)} %copy.42, f32[2816]{0:T(1024)S(1)} %get-tuple-element.181, f32[2816]{0:T(1024)S(1)} %get-tuple-element.182, f32[2816]{0:T(1024)S(1)} %get-tuple-element.180, f32[2816]{0:T(1024)S(1)} %get-tuple-element.179, ...), kind=kLoop, calls=%fused_computation.50 | loop fusion | flops 56229888 | bytes 8723968 | tf_op jit(solution)/shard_map/convert_element_type | solution.py:95
  338.5 0.8 fusion.47
  339.3 2.5 slice.72
  342.0 11.3 %reshape.79 = bf16[3,256,40,64]{1,0,3,2:T(4,128)(2,1)} reshape(bf16[768,2560]{0,1:T(8,128)(2,1)} %slice.72) | data formatting | bytes 7864320 | tf_op jit(solution)/shard_map/reshape | solution.py:97
  353.2 5.2 copy.44
  358.4 9.8 %while.33 = (s32[]{:T(128)}, f32[3,40,64,128]{3,2,1,0:T(8,128)}, bf16[3,256,40,64]{1,3,2,0:T(8,128)(2,1)}, f32[3,40,256]{2,1,0:T(8,128)S(1)}, f32[3,40,256]{2,0,...) while((s32[]{:T(128)}, f32[3,40,64,128]{3,2,1,0:T(8,128)}, bf16[3,256,40,64]{1,3,2,0:T(8,128)(2,1)}, ...), condition=%wide.region_4.5_spmd, body=%wide.region_3.4_spmd.sunk | while | flops 169758720 | bytes 3262517 | solution.py:111
  358.8 2.9 fusion.67
  362.1 2.9 fusion.67
  365.3 2.9 fusion.67
  368.2 4.7 while.35
  368.2 1.5 bitcast_add_fusion.6
  369.8 1.5 bitcast_add_fusion.6
  371.4 1.5 bitcast_add_fusion.6
  372.9 1.9 collective-permute-start.5
  374.9 17.0 %collective-permute-done.5 = f32[40,64,128]{2,1,0:T(8,128)S(1)} collective-permute-done((f32[40,64,128]{2,1,0:T(8,128)S(1)}, f32[40,64,128]{2,1,0:T(8,128)S(1)}, u32[]{:S(2)}, u32[]{:S(2)}) %collective-permute-start.5) | collective-permute-done | bytes 1310752 | tf_op jit(solution)/shard_map/ppermute | solution.py:43
  391.9 1.9 collective-permute-start.6
  393.8 2.2 collective-permute-start
  396.0 14.8 %collective-permute-done = f32[40]{0:T(128)S(1)} collective-permute-done((f32[40]{0:T(128)S(1)}, f32[40]{0:T(128)S(1)}, u32[]{:S(2)}, u32[]{:S(2)}) %collective-permute-start) | collective-permute-done | bytes 192 | tf_op jit(solution)/shard_map/ppermute | solution.py:43
  410.8 1.9 collective-permute-start.1
  412.7 2.9 collective-permute-done.1
  415.9 2.1 collective-permute-start.7
  418.1 28.6 %collective-permute-done.7 = f32[40,64,128]{2,1,0:T(8,128)S(1)} collective-permute-done((f32[40,64,128]{2,1,0:T(8,128)S(1)}, f32[40,64,128]{2,1,0:T(8,128)S(1)}, u32[]{:S(2)}, u32[]{:S(2)}) %collective-permute-start.7) | collective-permute-done | bytes 1310752 | tf_op jit(solution)/shard_map/ppermute | solution.py:43
  446.9 3.9 collective-permute-start.8
  450.8 2.1 collective-permute-start.2
  453.1 27.8 %collective-permute-done.2 = f32[40]{0:T(128)S(1)} collective-permute-done((f32[40]{0:T(128)S(1)}, f32[40]{0:T(128)S(1)}, u32[]{:S(2)}, u32[]{:S(2)}) %collective-permute-start.2) | collective-permute-done | bytes 192 | tf_op jit(solution)/shard_map/ppermute | solution.py:43
  481.0 1.1 copy.47
  482.1 1.3 multiply_add_fusion
  483.4 209.5 %while.34 = (s32[]{:T(128)}, f32[40,64,128]{2,1,0:T(8,128)}, f32[3,256,40,64]{1,0,3,2:T(4,128)}, f32[3,40]{1,0:T(4,128)S(1)}, f32[3,40,64,128]{3,2,1,0:T(8,128)}...) while((s32[]{:T(128)}, f32[40,64,128]{2,1,0:T(8,128)}, ...), condition=%wide.region_8.9_spmd, body=%wide.region_7.8_spmd.sunk | while | flops 1374093312 | bytes 26208364 | solution.py:127
  483.4 2.5 fusion.74
  486.2 4.3 fusion.76
  490.5 2.9 copy.76
  493.4 56.8 %dynamic_update_slice.12 = f32[3,256,40,64]{1,0,3,2:T(4,128)} dynamic-update-slice(f32[3,256,40,64]{1,0,3,2:T(4,128)} %get-tuple-element.412, f32[1,256,40,64]{1,0,3,2:T(1,128)S(1)} %copy.76, s32[]{:T(128)} %get-tuple-element.410, s32[]{:T(128)} %constant.52.clone.1..sunk, s32[]{:T(128)} %constant.52.clone.1..sunk, s32[]{:T(128)} %constant.52.clone.1..sunk) | dynamic-update-slice | bytes 5242884 | tf_op jit(solution)/shard_map/while/body/jit(dynamic_update_index_in_dim)/dynamic_update_slice | solution.py:127
  550.2 3.0 bitcast_add_fusion.5
  553.2 2.5 fusion.74
  556.0 4.3 fusion.76
  560.3 2.9 copy.76
  563.2 56.8 %dynamic_update_slice.12 = f32[3,256,40,64]{1,0,3,2:T(4,128)} dynamic-update-slice(f32[3,256,40,64]{1,0,3,2:T(4,128)} %get-tuple-element.412, f32[1,256,40,64]{1,0,3,2:T(1,128)S(1)} %copy.76, s32[]{:T(128)} %get-tuple-element.410, s32[]{:T(128)} %constant.52.clone.1..sunk, s32[]{:T(128)} %constant.52.clone.1..sunk, s32[]{:T(128)} %constant.52.clone.1..sunk) | dynamic-update-slice | bytes 5242884 | tf_op jit(solution)/shard_map/while/body/jit(dynamic_update_index_in_dim)/dynamic_update_slice | solution.py:127
  620.0 3.0 bitcast_add_fusion.5
  623.0 2.5 fusion.74
  625.8 4.3 fusion.76
  630.1 2.9 copy.76
  633.1 56.8 %dynamic_update_slice.12 = f32[3,256,40,64]{1,0,3,2:T(4,128)} dynamic-update-slice(f32[3,256,40,64]{1,0,3,2:T(4,128)} %get-tuple-element.412, f32[1,256,40,64]{1,0,3,2:T(1,128)S(1)} %copy.76, s32[]{:T(128)} %get-tuple-element.410, s32[]{:T(128)} %constant.52.clone.1..sunk, s32[]{:T(128)} %constant.52.clone.1..sunk, s32[]{:T(128)} %constant.52.clone.1..sunk) | dynamic-update-slice | bytes 5242884 | tf_op jit(solution)/shard_map/while/body/jit(dynamic_update_index_in_dim)/dynamic_update_slice | solution.py:127
  689.8 3.0 bitcast_add_fusion.5
  692.8 5.9 copy.63
  698.8 4.3 fusion.35
  703.0 6.3 copy.51
  (80 shorter events, 3.9 us)
Async XLA Ops:
  249.3 13.2 %copy-start.1 = (f32[1,40,768]{2,1,0:T(8,128)S(1)}, f32[1,40,768]{2,1,0:T(8,128)}, u32[]{:S(2)}) copy-start(f32[1,40,768]{2,1,0:T(8,128)} %param.13) | copy-start | bytes 368644
  249.3 15.4 %copy-start.2 = (bf16[4,2816]{1,0:T(4,128)(2,1)S(1)}, bf16[4,2816]{1,0:T(4,128)(2,1)}, u32[]{:S(2)}) copy-start(bf16[4,2816]{1,0:T(4,128)(2,1)} %param.15) | copy-start | bytes 67588
  262.5 12.8 %collective-permute-start.3 = (bf16[1408,2560]{1,0:T(8,128)(2,1)}, bf16[1408,2560]{1,0:T(8,128)(2,1)}, u32[]{:S(2)}, u32[]{:S(2)}) collective-permute-start(bf16[1408,2560]{1,0:T(8,128)(2,1)} %reshape.77), channel_id=1, source_target_pairs={{0,1},{1,0},{2,3},{3,2},{4,5},{5,4},{6,7},{7,6},{8,9},{9,8},{10,11... | collective-permute-start | bytes 21626888 | tf_op jit(solution)/shard_map/ppermute | solution.py:63
  265.0 10.3 %copy-start.5 = (bf16[1,768,2560]{2,1,0:T(8,128)(2,1)S(1)}, bf16[1,768,2560]{2,1,0:T(8,128)(2,1)}, u32[]{:S(2)}) copy-start(bf16[1,768,2560]{2,1,0:T(8,128)(2,1)} %param.12) | copy-start | bytes 11796484
  305.8 16.9 %collective-permute-start.4 = (bf16[3,2816]{1,0:T(4,128)(2,1)S(1)}, bf16[3,2816]{1,0:T(4,128)(2,1)S(1)}, u32[]{:S(2)}, u32[]{:S(2)}) collective-permute-start(bf16[3,2816]{1,0:T(4,128)(2,1)S(1)} %slice.52), channel_id=1, source_target_pairs={{0,1},{1,2},{2,3},{3,4},{4,5},{5,6},{6,7},{8,9},{9,10},{10,11},{11... | collective-permute-start | bytes 50696 | tf_op jit(solution)/shard_map/ppermute | solution.py:43
  315.0 8.1 %copy-start.3 = (f32[2816]{0:T(1024)S(1)}, f32[2816]{0:T(1024)}, u32[]{:S(2)}) copy-start(f32[2816]{0:T(1024)} %param.16) | copy-start | bytes 33796
  338.5 3.3 copy-start
  372.9 18.9 %collective-permute-start.5 = (f32[40,64,128]{2,1,0:T(8,128)S(1)}, f32[40,64,128]{2,1,0:T(8,128)S(1)}, u32[]{:S(2)}, u32[]{:S(2)}) collective-permute-start(f32[40,64,128]{2,1,0:T(8,128)S(1)} %get-tuple-element.112), channel_id=1, source_target_pairs={{0,1},{1,2},{2,3},{3,4},{4,5},{5,6},{6,7},{8,9},{9,10},{10,11},{11... | collective-permute-start | bytes 3932168 | tf_op jit(solution)/shard_map/ppermute | solution.py:43
  391.9 23.8 %collective-permute-start.6 = (f32[40,64,128]{2,1,0:T(8,128)S(1)}, f32[40,64,128]{2,1,0:T(8,128)S(1)}, u32[]{:S(2)}, u32[]{:S(2)}) collective-permute-start(f32[40,64,128]{2,1,0:T(8,128)S(1)} %collective-permute-done.5), channel_id=1, source_target_pairs={{0,1},{1,2},{2,3},{3,4},{4,5},{5,6},{6,7},{8,9},{9,10},{10,11},{11... | collective-permute-start | bytes 3932168 | tf_op jit(solution)/shard_map/ppermute | solution.py:43
  393.8 17.1 %collective-permute-start = (f32[40]{0:T(128)S(1)}, f32[40]{0:T(128)S(1)}, u32[]{:S(2)}, u32[]{:S(2)}) collective-permute-start(f32[40]{0:T(128)S(1)} %get-tuple-element.177), channel_id=1, source_target_pairs={{0,1},{1,2},{2,3},{3,4},{4,5},{5,6},{6,7},{8,9},{9,10},{10,11},{11... | collective-permute-start | bytes 488 | tf_op jit(solution)/shard_map/ppermute | solution.py:43
  410.8 4.8 collective-permute-start.1
  415.7 37.3 %copy-start.4 = (f32[40]{0:T(128)S(1)}, f32[40]{0:T(128)}, u32[]{:S(2)}) copy-start(f32[40]{0:T(128)} %param.17) | copy-start | bytes 484
  415.9 30.7 %collective-permute-start.7 = (f32[40,64,128]{2,1,0:T(8,128)S(1)}, f32[40,64,128]{2,1,0:T(8,128)S(1)}, u32[]{:S(2)}, u32[]{:S(2)}) collective-permute-start(f32[40,64,128]{2,1,0:T(8,128)S(1)} %multiply_add_fusion.2), channel_id=1, source_target_pairs={{0,2},{1,3},{2,4},{3,5},{4,6},{5,7},{8,10},{9,11},{10,12},{11,13},... | collective-permute-start | bytes 3932168 | tf_op jit(solution)/shard_map/ppermute | solution.py:43
  446.9 35.2 %collective-permute-start.8 = (f32[40,64,128]{2,1,0:T(8,128)S(1)}, f32[40,64,128]{2,1,0:T(8,128)S(1)}, u32[]{:S(2)}, u32[]{:S(2)}) collective-permute-start(f32[40,64,128]{2,1,0:T(8,128)S(1)} %multiply_add_fusion.1), channel_id=1, source_target_pairs={{0,4},{1,5},{2,6},{3,7},{8,12},{9,13},{10,14},{11,15},{16,20},{17,... | collective-permute-start | bytes 3932168 | tf_op jit(solution)/shard_map/ppermute | solution.py:43
  450.8 30.1 %collective-permute-start.2 = (f32[40]{0:T(128)S(1)}, f32[40]{0:T(128)S(1)}, u32[]{:S(2)}, u32[]{:S(2)}) collective-permute-start(f32[40]{0:T(128)S(1)} %get-tuple-element.226), channel_id=1, source_target_pairs={{0,2},{1,3},{2,4},{3,5},{4,6},{5,7},{8,10},{9,11},{10,12},{11,13},... | collective-permute-start | bytes 488 | tf_op jit(solution)/shard_map/ppermute | solution.py:43
